TPU v7x, 32 devices: a whole 2x2x4 slice. The times are simulated.
32 devices in a mesh: groups: 2 (over y), wide: 4 (over z), ctx: 4 (over x, core).
Axes of the slice: x: 2, y: 2, z: 4, core: 2. Of those that a mesh axis runs over, the one named last changes fastest.
Arguments:
- queries: bfloat16 [4096, 6144], P(('groups', 'ctx'), 'wide'), parts along dimension 0, may hold values from -48 to 48
- key_rows: bfloat16 [4096, 1024], P(('groups', 'ctx')), parts along dimension 0, may hold values from -48 to 48
- value_head_rows: bfloat16 [4096, 1024], P(('groups', 'ctx')), parts along dimension 0, may hold values from -18 to 18
- residual: bfloat16 [4096, 6144], P(('groups', 'ctx'), 'wide'), parts along dimension 0, may hold values from -48 to 48
- out_weight: bfloat16 [6144, 6144], P('wide'), may hold values from -0.109375 to 0.109375
- norm_gain: bfloat16 [6144], P('wide'), may hold values from 0.25 to 1.75
- router_weight: bfloat16 [6144, 8], P('wide'), may hold values from -0.078125 to 0.078125
- gate_weight: bfloat16 [6144, 8192], P('wide', 'ctx'), may hold values from -0.078125 to 0.078125
- up_weight: bfloat16 [6144, 8192], P('wide', 'ctx'), may hold values from -0.078125 to 0.078125
- down_weight: bfloat16 [8192, 6144], P('ctx', 'wide'), may hold values from -0.0625 to 0.0625
- expert_ids: int32 [4096, 2], P('groups'), parts along dimension 0, may hold values from 0 to 7, as said below
- slot_ids: int32 [4096, 2], P('groups'), parts along dimension 0, may hold values from -1 to 639, as said below
Outputs:
- layer_out: bfloat16 [4096, 6144], P(('groups', 'ctx'), 'wide'), parts along dimension 0
There are 2 independent parts, one for each index of `groups`. A program takes and returns all parts, laid end to end along the dimension named above; an argument that names none is the same for every part. Nothing has to cross between parts.
Inputs may be any that keep to these rules, and one draw needn't show every extreme that they name: `expert_ids`: each row names 2 different experts; expert 0 is named by at least 704 rows, so its buffer is full in every draw. `slot_ids`: the rows naming one expert take its buffer rows 0, 1, 2 and so on in the order of positions (for one position, the earlier column first); once 640 rows are taken, further choices of that expert hold -1. Rows of one expert's buffer are never shared.
All inputs are finite; a program needn't handle non-finite values.
Results may differ from a plain program's by a relative error of at most 0.015.
Values may be sent and summed in bfloat16 or wider, within the bound.
No kernel may reach another device: no remote copies, remote signals or barrier semaphores. Data moves between devices by JAX's collectives and lax.ppermute only.
A program may use at most 192 MiB of HBM per device.

v0:
```python
import math
import jax
import jax.numpy as jnp
from jax import lax
from jax.sharding import PartitionSpec as P

D = 6144
QUERY_HEADS = 48
KEY_VALUE_HEADS = 8
HEAD_SIZE = 128
NEG_FILL = -1e30
EPSILON = 1e-05


def token_slots(expert_ids, slot_ids, capacity):
    in_window = jnp.logical_and(expert_ids == 0, slot_ids >= 0)
    picked = jnp.max(jnp.where(in_window, slot_ids, -1), axis=1)
    return jnp.where(picked >= 0, picked, capacity)


def other_experts(expert_ids, slot_of_token, capacity):
    partner = jnp.sum(expert_ids, axis=1)
    return jnp.zeros((capacity,), jnp.int32).at[slot_of_token].set(partner, mode="drop")


def expert_hidden(gate_sum, up_sum, square_sum, logit_sum, slot_other, model_width):
    inverse_rms = lax.rsqrt(square_sum / model_width + EPSILON)
    gate_value = gate_sum * inverse_rms[:, None]
    up_value = up_sum * inverse_rms[:, None]
    logit_value = logit_sum * inverse_rms[:, None]
    columns = jnp.arange(logit_value.shape[1], dtype=jnp.int32)
    partner_logit = jnp.sum(
        jnp.where(columns[None, :] == slot_other[:, None], logit_value, 0.0), axis=1
    )
    mixing = jax.nn.sigmoid(logit_value[:, 0] - partner_logit)
    return (jax.nn.silu(gate_value) * up_value * mixing[:, None]).astype(jnp.bfloat16)


def local(
    queries,
    key_rows,
    value_head_rows,
    residual,
    out_weight,
    norm_gain,
    router_weight,
    gate_weight,
    up_weight,
    down_weight,
    expert_ids,
    slot_ids,
):
    ctx_count = lax.axis_size("ctx")
    wide_index = lax.axis_index("wide")
    ctx_index = lax.axis_index("ctx")
    rows_local = queries.shape[0]
    heads_local = queries.shape[1] // HEAD_SIZE
    query_group_width = QUERY_HEADS // KEY_VALUE_HEADS
    shared_heads = max(1, heads_local // query_group_width)
    per_shared = heads_local // shared_heads
    first_shared = wide_index * heads_local // query_group_width
    key_used = lax.dynamic_slice_in_dim(
        key_rows, first_shared * HEAD_SIZE, shared_heads * HEAD_SIZE, 1
    )
    value_used = lax.dynamic_slice_in_dim(
        value_head_rows, first_shared * HEAD_SIZE, shared_heads * HEAD_SIZE, 1
    )
    query_blocks = queries.reshape(rows_local, shared_heads, per_shared, HEAD_SIZE)
    query_pos = ctx_index * rows_local + jnp.arange(rows_local, dtype=jnp.int32)
    last_query = ctx_index * rows_local + rows_local - 1
    scale_factor = 1.0 / math.sqrt(HEAD_SIZE)
    start_state = (
        jnp.full((shared_heads, per_shared, rows_local), -jnp.inf, jnp.float32),
        jnp.zeros((shared_heads, per_shared, rows_local), jnp.float32),
        jnp.zeros((shared_heads, per_shared, rows_local, HEAD_SIZE), jnp.float32),
    )
    pieces = (
        lax.all_gather(key_used, "ctx", axis=0, tiled=True),
        lax.all_gather(value_used, "ctx", axis=0, tiled=True),
    )

    def update(state):
        running_max, running_sum, running_acc = state
        key_piece = pieces[0].reshape(-1, shared_heads, HEAD_SIZE)
        value_piece = pieces[1].reshape(-1, shared_heads, HEAD_SIZE)
        scores = (
            jnp.einsum(
                "skqd,rkd->kqsr", query_blocks, key_piece, preferred_element_type=jnp.float32
            )
            * scale_factor
        )
        key_pos = jnp.arange(key_piece.shape[0], dtype=jnp.int32)
        allowed = (key_pos[None, :] <= query_pos[:, None])[None, None, :, :]
        masked = jnp.where(allowed, scores, NEG_FILL)
        new_max = jnp.max(masked, axis=-1)
        weights = jnp.where(allowed, jnp.exp(masked - new_max[..., None]), 0.0)
        decay = jnp.exp(running_max - new_max)
        new_sum = running_sum * decay + jnp.sum(weights, axis=-1)
        added = jnp.einsum(
            "kqsr,rkd->kqsd",
            weights.astype(jnp.bfloat16),
            value_piece,
            preferred_element_type=jnp.float32,
        )
        return (new_max, new_sum, running_acc * decay[..., None] + added)

    final_max, final_sum, final_acc = lax.cond(
        jnp.int32(0) > last_query, lambda state: state, update, start_state
    )
    attended = final_acc / final_sum[..., None]
    attended = (
        jnp.transpose(attended, (2, 0, 1, 3))
        .reshape(rows_local, heads_local * HEAD_SIZE)
        .astype(jnp.bfloat16)
    )
    partial_out = jnp.dot(attended, out_weight, preferred_element_type=jnp.float32)
    head_sum = lax.psum_scatter(
        partial_out.astype(jnp.bfloat16), "wide", scatter_dimension=1, tiled=True
    ).astype(jnp.float32)
    resid = (residual.astype(jnp.float32) + head_sum).astype(jnp.bfloat16)
    seq_len = rows_local * ctx_count
    capacity = seq_len * 5 // 16
    width_local = resid.shape[1]
    slot_of_token = token_slots(expert_ids, slot_ids, capacity)
    slot_other = other_experts(expert_ids, slot_of_token, capacity)
    buffer = (
        jnp.zeros((capacity, width_local), jnp.bfloat16)
        .at[slot_of_token]
        .set(lax.all_gather(resid, "ctx", axis=0, tiled=True), mode="drop")
    )
    buffer_wide = buffer.astype(jnp.float32)
    square_part = jnp.sum(buffer_wide * buffer_wide, axis=1)
    scaled = (buffer_wide * norm_gain.astype(jnp.float32)[None, :]).astype(jnp.bfloat16)
    gate_part = jnp.dot(scaled, gate_weight, preferred_element_type=jnp.float32)
    up_part = jnp.dot(scaled, up_weight, preferred_element_type=jnp.float32)
    logit_part = jnp.dot(scaled, router_weight, preferred_element_type=jnp.float32)
    gate_sum, up_sum, square_sum, logit_sum = (
        lax.psum(gate_part.astype(jnp.bfloat16), "wide").astype(jnp.float32),
        lax.psum(up_part.astype(jnp.bfloat16), "wide").astype(jnp.float32),
        lax.psum(square_part.astype(jnp.bfloat16), "wide").astype(jnp.float32),
        lax.psum(logit_part.astype(jnp.bfloat16), "wide").astype(jnp.float32),
    )
    hidden = expert_hidden(gate_sum, up_sum, square_sum, logit_sum, slot_other, D)
    expert_part = jnp.dot(hidden, down_weight, preferred_element_type=jnp.float32)
    expert_pad = jnp.concatenate([expert_part, jnp.zeros((1, width_local), jnp.float32)], axis=0)
    moe_rows = lax.psum_scatter(
        jnp.take(expert_pad, slot_of_token, axis=0).astype(jnp.bfloat16),
        "ctx",
        scatter_dimension=0,
        tiled=True,
    ).astype(jnp.float32)
    return (resid.astype(jnp.float32) + moe_rows).astype(jnp.bfloat16)


def solution(mesh):
    placed = (
        P(("groups", "ctx"), "wide"),
        P(("groups", "ctx"), None),
        P(("groups", "ctx"), None),
        P(("groups", "ctx"), "wide"),
        P("wide", None),
        P("wide"),
        P("wide", None),
        P("wide", "ctx"),
        P("wide", "ctx"),
        P("ctx", "wide"),
        P("groups", None),
        P("groups", None),
    )
    return jax.shard_map(
        local, mesh=mesh, in_specs=placed, out_specs=P(("groups", "ctx"), "wide"), check_vma=False
    )
```

profile of v0, /device:TPU:0, one launch (start us, length us, event | category | flops | bytes accessed | tf_op | source)
XLA Modules:
  0.0 613.0 jit_solution(8369827461181199514)
XLA Ops:
  6.5 1.2 copy-done
  7.8 0.7 constant_dynamic-slice_fusion.1
  8.5 0.0 all-gather.4.cloned.1.call-update
  8.5 0.0 all-gather.6.cloned.1.call-start
  8.6 1.7 constant_dynamic-slice_fusion
  10.2 0.0 all-gather.6.cloned.1.call-update
  10.3 0.0 reduce-scatter.3.cloned.1.call-start
  10.3 18.0 %all-gather.4.cloned.1.call-done = bf16[2048,256]{1,0:T(8,128)(2,1)} async-done(((bf16[512,256]{1,0:T(8,128)(2,1)}), bf16[2048,256]{1,0:T(8,128)(2,1)}) %all-gather.4.cloned.1.call-update) | async-done | bytes 1048592 | tf_op jit(solution)/shard_map/all_gather | solution.py:78
  28.3 18.3 %all-gather.6.cloned.1.call-done = bf16[2048,256]{1,0:T(8,128)(2,1)} async-done(((bf16[512,256]{1,0:T(8,128)(2,1)}), bf16[2048,256]{1,0:T(8,128)(2,1)}) %all-gather.6.cloned.1.call-update) | async-done | bytes 1048592 | tf_op jit(solution)/shard_map/all_gather | solution.py:79
  46.6 75.7 %conditional.1 = (f32[2,6,512]{2,1,0:T(8,128)S(1)}, f32[2,6,512,128]{2,3,1,0:T(8,128)}) conditional(s32[]{:T(128)} %convert_element_type.76, (s32[]{:T(128)}, s32[512]{0:T(512)S(1)}, bf16[2048,256]{1,0:T(8,128)(2,1)}, bf16[512,1536]{1,0:T(8,128)(2,1)}, bf16[2048,256]{1,0:T(8,128)(2,1)}) %tuple.13, () %tuple.14), branch_computations={%region_0.3_spmd, %region_3.4_spmd} | conditional | flops 6607870464 | bytes 180058160 | solution.py:107
  46.6 0.8 iota_compare_fusion
  47.5 1.7 copy.28
  49.2 2.1 reshape.71
  51.3 21.1 %fusion = (f32[2,6,512]{2,1,0:T(8,128)S(1)}, f32[2,2048,512,6]{2,1,3,0:T(8,128)}) fusion(pred[512,2048]{0,1:T(8,128)(4,1)S(1)} %iota_compare_fusion, bf16[512,2,6,128]{0,3,2,1:T(8,128)(2,1)S(1)} %bitcast.29, bf16[2048,2,128,1]{2,1,0,3:T(2,128)(2,1)} %bitcast.30), kind=kOutput, calls=%fused_computation.5 | convolution fusion | flops 3258968064 | bytes 54026240 | tf_op jit(solution)/shard_map/cond/branch_0_fun/skqd,rkd->kqsr/dot_general | solution.py:87
  72.4 22.0 %fusion.2 = f32[2,6,512]{2,1,0:T(8,128)S(1)} fusion(f32[2,2048,512,6]{2,1,3,0:T(8,128)} %get-tuple-element.49, f32[2,6,512]{2,1,0:T(8,128)S(1)} %get-tuple-element.48, pred[512,2048]{0,1:T(8,128)(4,1)S(1)} %iota_compare_fusion), kind=kLoop, calls=%fused_computation.7 | loop fusion | flops 62908416 | bytes 51429376 | tf_op jit(solution)/shard_map/cond/branch_0_fun/reduce_sum | solution.py:98
  94.4 0.3 reshape.73
  94.7 24.0 %fusion.6 = f32[2,6,512,128]{3,2,1,0:T(8,128)} fusion(f32[2,2048,512,6]{2,1,3,0:T(8,128)} %get-tuple-element.49, f32[2,6,512]{2,1,0:T(8,128)S(1)} %get-tuple-element.48, pred[512,2048]{0,1:T(8,128)(4,1)S(1)} %iota_compare_fusion, f32[2,6,512]{2,1,0:T(8,128)S(1)} %get-tuple-element.46, bf16[2048,2,128,1]{2,1,0,3:T(2,128)(2,1)S(1)} %bitcast.32), kind=kOutput, calls=%fused_computation.11 | convolution fusion | flops 3284926464 | bytes 55623680 | tf_op jit(solution)/shard_map/cond/branch_0_fun/kqsr,rkd->kqsd/dot_general | solution.py:99
  118.8 3.5 copy.38
  122.3 2.3 divide_convert_fusion
  124.7 15.7 %convolution_convert_fusion = bf16[512,6144]{1,0:T(8,128)(2,1)} fusion(bf16[512,1536]{0,1:T(8,128)(2,1)S(1)} %bitcast.31, bf16[1536,6144]{1,0:T(8,128)(2,1)} %param.18), kind=kOutput, calls=%fused_computation.22 | convolution fusion | flops 9666822144 | bytes 26738688 | tf_op jit(solution)/shard_map/dot_general | solution.py:116
  140.3 0.0 reduce-scatter.3.cloned.1.call-update
  140.4 0.0 copy-start.7
  140.4 0.0 copy-start.5
  140.4 0.0 copy-start.6
  140.4 0.0 all-gather.8.cloned.1.call-start
  140.5 110.8 %reduce-scatter.3.cloned.1.call-done = bf16[512,1536]{1,0:T(8,128)(2,1)} async-done(((bf16[512,6144]{1,0:T(8,128)(2,1)}), bf16[512,1536]{1,0:T(8,128)(2,1)}) %reduce-scatter.3.cloned.1.call-update) | async-done | bytes 1572880 | tf_op jit(solution)/shard_map/reduce_scatter | solution.py:117
  251.3 2.9 add_convert_fusion.1
  254.2 0.0 all-gather.8.cloned.1.call-update
  254.3 0.0 all-reduce.5.cloned.1.call-start
  254.4 0.1 fusion.33
  254.4 46.9 %all-gather.8.cloned.1.call-done = bf16[2048,1536]{1,0:T(8,128)(2,1)} async-done(((bf16[512,1536]{1,0:T(8,128)(2,1)}), bf16[2048,1536]{1,0:T(8,128)(2,1)}) %all-gather.8.cloned.1.call-update) | async-done | bytes 6291472 | tf_op jit(solution)/shard_map/all_gather | solution.py:129
  301.3 11.4 %scatter_custom_fusion = bf16[640,1536]{1,0:T(8,128)(2,1)S(1)} fusion(s32[2048]{0:T(1024)S(1)} %bitcast.35, bf16[2048,1536]{1,0:T(8,128)(2,1)} %all-gather.8.cloned.1.call-done, bf16[]{:T(256)} %constant.48.clone.1), kind=kCustom, calls=%fused_computation.36 | custom fusion | bytes 1966592 | tf_op jit(solution)/shard_map/scatter | solution.py:129
  312.8 8.5 %convolution_convert_fusion.1 = bf16[640,2048]{1,0:T(8,128)(2,1)} fusion(bf16[1536,2048]{1,0:T(8,128)(2,1)} %param.22, bf16[640,1536]{1,0:T(8,128)(2,1)S(1)} %scatter_custom_fusion, f32[1536]{0:T(1024)S(1)} %convert_element_type.85), kind=kOutput, calls=%fused_computation.28 | convolution fusion | flops 4030791680 | bytes 10885120 | tf_op jit(solution)/shard_map/dot_general | solution.py:135
  321.2 8.2 %convolution_convert_fusion.2 = bf16[640,2048]{1,0:T(8,128)(2,1)} fusion(bf16[1536,2048]{1,0:T(8,128)(2,1)} %param.21, bf16[640,1536]{1,0:T(8,128)(2,1)S(1)} %scatter_custom_fusion, f32[1536]{0:T(1024)S(1)} %convert_element_type.85), kind=kOutput, calls=%fused_computation.29 | convolution fusion | flops 4030791680 | bytes 10885120 | tf_op jit(solution)/shard_map/dot_general | solution.py:134
  329.5 0.0 all-reduce.5.cloned.1.call-update
  329.5 0.0 reduce-scatter.5.cloned.1.call-start
  329.6 8.0 %scatter_custom_fusion.1 = s32[640]{0:T(1024)S(1)} fusion(s32[2048]{0:T(1024)S(1)} %bitcast.36, s32[2048]{0:T(1024)S(1)} %get-tuple-element.40, s32[]{:T(128)} %constant.22.clone.1), kind=kCustom, calls=%fused_computation.54 | custom fusion | bytes 2564 | tf_op jit(solution)/shard_map/scatter | solution.py:23
  337.7 0.5 fusion.17
  338.1 0.6 fusion.23
  338.7 19.9 %all-reduce.1 = (bf16[640]{0:T(1024)(128)(2,1)S(1)}, bf16[640,8]{0,1:T(8,128)(2,1)S(1)}) all-reduce(bf16[640]{0:T(1024)(128)(2,1)S(1)} %fusion.17, bf16[640,8]{0,1:T(8,128)(2,1)S(1)} %fusion.23), channel_id=1, replica_groups=mesh['groups'=2,'wide'=4,'ctx'=4] {'wide'}, use_global_device_ids=true, to_apply=%region_9.10 | all-reduce | flops 5760 | bytes 23040 | tf_op jit(solution)/shard_map/psum | solution.py:140
  358.7 160.5 %all-reduce.5.cloned.1.call-done = (bf16[640,2048]{1,0:T(8,128)(2,1)}, bf16[640,2048]{1,0:T(8,128)(2,1)}) async-done(((bf16[640,2048]{1,0:T(8,128)(2,1)}, bf16[640,2048]{1,0:T(8,128)(2,1)}), (bf16[640,2048]{1,0:T(8,128)(2,1)}, bf16[640,2048]{1,0:T(8,128)(2,1)})) %all-reduce.5.cloned.1.call-update) | async-done | bytes 5242896 | tf_op jit(solution)/shard_map/psum | solution.py:139
  519.2 9.2 %fusion.18 = bf16[640,1536]{1,0:T(8,128)(2,1)S(1)} fusion(bf16[2048,1536]{1,0:T(8,128)(2,1)} %param.23, bf16[640,2048]{1,0:T(8,128)(2,1)} %get-tuple-element.44, bf16[640,2048]{1,0:T(8,128)(2,1)} %get-tuple-element.45, f32[640]{0:T(1024)S(1)} %divide_reduce_fusion, f32[640]{0:T(1024)S(1)} %add_rsqrt_fusion), kind=kOutput, calls=%fused_computation.33 | convolution fusion | flops 4040949760 | bytes 13505536 | tf_op jit(solution)/shard_map/dot_general | solution.py:144
  528.4 0.1 concatenate.3
  528.5 10.1 %gather_fusion = bf16[2048,1536]{1,0:T(8,128)(2,1)} fusion(bf16[641,1536]{1,0:T(8,128)(2,1)S(1)} %concatenate.3, s32[2048]{0:T(1024)S(1)} %broadcast_clamp_fusion), kind=kCustom, calls=%fused_computation | custom fusion | bytes 12591104 | tf_op jit(solution)/shard_map/jit(_take)/gather | solution.py:147
  538.7 6.6 %select_convert_fusion = bf16[2048,1536]{1,0:T(8,128)(2,1)} fusion(bf16[2048,1536]{1,0:T(8,128)(2,1)} %gather_fusion, pred[2048]{0:T(1024)(128)(4,1)S(1)} %compare_and_fusion), kind=kLoop, calls=%fused_computation.21 | loop fusion | flops 3145728 | bytes 12584960 | tf_op jit(solution)/shard_map/convert_element_type | solution.py:147
  545.3 0.0 reduce-scatter.5.cloned.1.call-update
  545.3 58.0 %reduce-scatter.5.cloned.1.call-done = bf16[512,1536]{1,0:T(8,128)(2,1)} async-done(((bf16[2048,1536]{1,0:T(8,128)(2,1)}), bf16[512,1536]{1,0:T(8,128)(2,1)}) %reduce-scatter.5.cloned.1.call-update) | async-done | bytes 1572880 | tf_op jit(solution)/shard_map/reduce_scatter | solution.py:146
  603.2 2.9 add_convert_fusion
  (25 shorter events, 0.1 us)
Async XLA Ops:
  6.5 1.2 copy-start
  6.5 21.8 %all-gather.4.cloned.1.call-start = ((), (), s32[]{:S(2)}) async-start(), calls=%async_computation.2 | async-start | bytes 1310720 | tf_op jit(solution)/shard_map/all_gather | solution.py:78
  8.5 38.1 %all-gather.6.cloned.1.call-start = ((), (), s32[]{:S(2)}) async-start(), calls=%async_computation.3 | async-start | bytes 1310720 | tf_op jit(solution)/shard_map/all_gather | solution.py:79
  10.3 241.0 %reduce-scatter.3.cloned.1.call-start = ((), (), s32[]{:S(2)}) async-start(), calls=%async_computation.4 | async-start | bytes 7864320 | tf_op jit(solution)/shard_map/reduce_scatter | solution.py:117
  72.4 22.0 %copy-start.4 = (bf16[2048,256]{1,0:T(8,128)(2,1)S(1)}, bf16[2048,256]{1,0:T(8,128)(2,1)}, u32[]{:S(2)}) copy-start(bf16[2048,256]{1,0:T(8,128)(2,1)} %get-tuple-element.22) | copy-start | bytes 3145732 | tf_op jit(solution)/shard_map/cond
  140.3 111.0 %copy-start.3 = (bf16[512,1536]{1,0:T(8,128)(2,1)S(1)}, bf16[512,1536]{1,0:T(8,128)(2,1)}, u32[]{:S(2)}) copy-start(bf16[512,1536]{1,0:T(8,128)(2,1)} %param.17) | copy-start | bytes 4718596
  140.4 113.9 %copy-start.7 = (bf16[1536]{0:T(1024)(128)(2,1)S(1)}, bf16[1536]{0:T(1024)(128)(2,1)}, u32[]{:S(2)}) copy-start(bf16[1536]{0:T(1024)(128)(2,1)} %param.19) | copy-start | bytes 9220
  140.4 114.0 %copy-start.5 = (s32[2048,2]{0,1:T(2,128)S(1)}, s32[2048,2]{0,1:T(2,128)}, u32[]{:S(2)}) copy-start(s32[2048,2]{0,1:T(2,128)} %param.24) | copy-start | bytes 49156
  140.4 114.0 %copy-start.6 = (s32[2048,2]{0,1:T(2,128)S(1)}, s32[2048,2]{0,1:T(2,128)}, u32[]{:S(2)}) copy-start(s32[2048,2]{0,1:T(2,128)} %param.25) | copy-start | bytes 49156
  140.4 160.9 %all-gather.8.cloned.1.call-start = ((), (), s32[]{:S(2)}) async-start(), calls=%async_computation.5 | async-start | bytes 7864320 | tf_op jit(solution)/shard_map/all_gather | solution.py:129
  254.3 264.9 %all-reduce.5.cloned.1.call-start = ((), (), s32[]{:S(2)}) async-start(), calls=%async_computation.7 | async-start | bytes 10485760 | tf_op jit(solution)/shard_map/psum | solution.py:139
  329.5 8.6 %copy-start.8 = (bf16[1536,8]{0,1:T(8,128)(2,1)S(1)}, bf16[1536,8]{0,1:T(8,128)(2,1)}, u32[]{:S(2)}) copy-start(bf16[1536,8]{0,1:T(8,128)(2,1)} %param.20) | copy-start | bytes 73732
  329.5 273.7 %reduce-scatter.5.cloned.1.call-start = ((), (), s32[]{:S(2)}) async-start(), calls=%async_computation.6 | async-start | bytes 7864320 | tf_op jit(solution)/shard_map/reduce_scatter | solution.py:146
  545.3 58.0 %copy-start.2 = (bf16[512,1536]{1,0:T(8,128)(2,1)S(1)}, bf16[512,1536]{1,0:T(8,128)(2,1)}, u32[]{:S(2)}) copy-start(bf16[512,1536]{1,0:T(8,128)(2,1)} %add_convert_fusion.1) | copy-start | bytes 4718596
  545.3 60.9 %copy-start.1 = (bf16[512,1024]{1,0:T(8,128)(2,1)S(1)}, bf16[512,1024]{1,0:T(8,128)(2,1)}, u32[]{:S(2)}) copy-start(bf16[512,1024]{1,0:T(8,128)(2,1)} %param.15) | copy-start | bytes 3145732
Sparse Core Ops, SparseCore 0:
  8.9 19.4 all-gather.3
  29.9 16.6 all-gather.5
  140.5 110.7 reduce-scatter.2
  254.4 46.8 all-gather.7
  329.6 189.4 all-reduce.4
  545.4 57.7 reduce-scatter.4
where the time goes:
time: 614 us; the launch traced here: 613 us
  waiting for transfers between devices  413 us (67%)
  matrix products  87.4 us (14%)
  local copies, waits for them, and re-layouts  41.1 us (7%)
  other arithmetic  38.2 us (6%)
  blocking collectives  19.9 us (3%)
  between operations  13.6 us (2%)
    psum x1, waiting for transfers between devices, local(): lax.psum(up_part.astype(jnp.bfloat16), 'wide').astype(jnp.float32)  160 us
    reduce_scatter x1, waiting for transfers between devices, local(): lax.psum_scatter(partial_out.astype(jnp.bfloat16), 'wide', scatter_dimens...  111 us
    reduce_scatter x1, waiting for transfers between devices, local(): lax.psum_scatter(jnp.take(expert_pad, slot_of_token, axis=0).astype(jnp.b...  58 us
    all_gather x1, waiting for transfers between devices, local(): lax.all_gather(resid, 'ctx', axis=0, tiled=True)  46.9 us
    dot_general x1, matrix products, update(): jnp.einsum('kqsr,rkd->kqsd', weights.astype(jnp.bfloat16), value_piece, p...  24 us
    reduce_sum x1, other arithmetic, update(): new_sum = running_sum * decay + jnp.sum(weights, axis=-1)  22 us
    dot_general x1, matrix products, update(): jnp.einsum('skqd,rkd->kqsr', query_blocks, key_piece, preferred_element_t...  21.1 us
    psum x1, blocking collectives, local(): lax.psum(square_part.astype(jnp.bfloat16), 'wide').astype(jnp.float32)  19.9 us
  transfers between devices with their start and end apart: 6, of which 6 were waited for; matrix products, arithmetic and copies ran while one was open for 2% of the time, Pallas kernels for 0%

commit v1 on v0

--- a/solution.py
+++ b/solution.py
@@ -136,7 +136,7 @@
     logit_part = jnp.dot(scaled, router_weight, preferred_element_type=jnp.float32)
     gate_sum, up_sum, square_sum, logit_sum = (
         lax.psum(gate_part.astype(jnp.bfloat16), "wide").astype(jnp.float32),
-        lax.psum(up_part.astype(jnp.bfloat16), "wide").astype(jnp.float32),
+        jnp.sum(lax.all_gather(up_part.astype(jnp.bfloat16), "wide"), axis=0).astype(jnp.float32),
         lax.psum(square_part.astype(jnp.bfloat16), "wide").astype(jnp.float32),
         lax.psum(logit_part.astype(jnp.bfloat16), "wide").astype(jnp.float32),
     )

time: 614 us -> 715 us (1.16); the launches traced: 613 us -> 705 us
  waiting for transfers between devices: 413 us -> 487 us
  other arithmetic: 38.2 us -> 46.9 us
  blocking collectives: 19.9 us -> 28.1 us
    all_gather x0 -> x1, waiting for transfers between devices: none -> 139 us  [local(): lax.all_gather(up_part.astype(jnp.bfloat16), 'wide')]
    psum x1, waiting for transfers between devices: 160 us -> 95.9 us  [local(): lax.psum(gate_part.astype(jnp.bfloat16), 'wide').astype(jnp.float32)]
    reduce_sum x0 -> x1, other arithmetic: none -> 8.71 us  [local(): jnp.sum(lax.all_gather(up_part.astype(jnp.bfloat16), 'wide'), axis=0)]
    psum x1, blocking collectives: 19.9 us -> 28.1 us  [local(): lax.psum(square_part.astype(jnp.bfloat16), 'wide').astype(jnp.float32)]
  transfers between devices with their start and end apart: 6 -> 7, of which waited for: 6 -> 7; matrix products, arithmetic and copies ran while one was open for 2% -> 4% of each run, Pallas kernels for 0% -> 0%
where the time goes in v1:
time: 715 us; the launch traced here: 705 us
  waiting for transfers between devices  487 us (68%)
  matrix products  87.4 us (12%)
  other arithmetic  46.9 us (7%)
  local copies, waits for them, and re-layouts  41.2 us (6%)
  blocking collectives  28.1 us (4%)
  between operations  14 us (2%)
    all_gather x1, waiting for transfers between devices, local(): lax.all_gather(up_part.astype(jnp.bfloat16), 'wide')  139 us
    reduce_scatter x1, waiting for transfers between devices, local(): lax.psum_scatter(partial_out.astype(jnp.bfloat16), 'wide', scatter_dimens...  111 us
    psum x1, waiting for transfers between devices, local(): lax.psum(gate_part.astype(jnp.bfloat16), 'wide').astype(jnp.float32)  95.9 us
    reduce_scatter x1, waiting for transfers between devices, local(): lax.psum_scatter(jnp.take(expert_pad, slot_of_token, axis=0).astype(jnp.b...  58 us
    all_gather x1, waiting for transfers between devices, local(): lax.all_gather(resid, 'ctx', axis=0, tiled=True)  46.9 us
    psum x1, blocking collectives, local(): lax.psum(square_part.astype(jnp.bfloat16), 'wide').astype(jnp.float32)  28.1 us
    dot_general x1, matrix products, update(): jnp.einsum('kqsr,rkd->kqsd', weights.astype(jnp.bfloat16), value_piece, p...  24.1 us
    reduce_sum x1, other arithmetic, update(): new_sum = running_sum * decay + jnp.sum(weights, axis=-1)  22 us
  transfers between devices with their start and end apart: 7, of which 7 were waited for; matrix products, arithmetic and copies ran while one was open for 4% of the time, Pallas kernels for 0%

profile of v1, /device:TPU:0, one launch (start us, length us, event | category | flops | bytes accessed | tf_op | source)
XLA Modules:
  0.0 704.6 jit_solution(2383391896233256260)
XLA Ops:
  6.5 1.2 copy-done
  7.8 0.7 constant_dynamic-slice_fusion.1
  8.5 0.0 all-gather.6.cloned.1.call-update
  8.5 0.0 all-gather.8.cloned.1.call-start
  8.6 1.7 constant_dynamic-slice_fusion
  10.2 0.0 all-gather.8.cloned.1.call-update
  10.3 0.0 reduce-scatter.3.cloned.1.call-start
  10.3 18.0 %all-gather.6.cloned.1.call-done = bf16[2048,256]{1,0:T(8,128)(2,1)} async-done(((bf16[512,256]{1,0:T(8,128)(2,1)}), bf16[2048,256]{1,0:T(8,128)(2,1)}) %all-gather.6.cloned.1.call-update) | async-done | bytes 1048592 | tf_op jit(solution)/shard_map/all_gather | solution.py:78
  28.3 18.3 %all-gather.8.cloned.1.call-done = bf16[2048,256]{1,0:T(8,128)(2,1)} async-done(((bf16[512,256]{1,0:T(8,128)(2,1)}), bf16[2048,256]{1,0:T(8,128)(2,1)}) %all-gather.8.cloned.1.call-update) | async-done | bytes 1048592 | tf_op jit(solution)/shard_map/all_gather | solution.py:79
  46.6 75.8 %conditional.1 = (f32[2,6,512]{2,1,0:T(8,128)S(1)}, f32[2,6,512,128]{2,3,1,0:T(8,128)}) conditional(s32[]{:T(128)} %convert_element_type.78, (s32[]{:T(128)}, s32[512]{0:T(512)S(1)}, bf16[2048,256]{1,0:T(8,128)(2,1)}, bf16[512,1536]{1,0:T(8,128)(2,1)}, bf16[2048,256]{1,0:T(8,128)(2,1)}) %tuple.13, () %tuple.14), branch_computations={%region_0.3_spmd, %region_3.4_spmd} | conditional | flops 6607870464 | bytes 180058160 | solution.py:107
  46.6 0.8 iota_compare_fusion
  47.5 1.7 copy.28
  49.2 2.1 reshape.71
  51.3 21.1 %fusion = (f32[2,6,512]{2,1,0:T(8,128)S(1)}, f32[2,2048,512,6]{2,1,3,0:T(8,128)}) fusion(pred[512,2048]{0,1:T(8,128)(4,1)S(1)} %iota_compare_fusion, bf16[512,2,6,128]{0,3,2,1:T(8,128)(2,1)S(1)} %bitcast.31, bf16[2048,2,128,1]{2,1,0,3:T(2,128)(2,1)} %bitcast.32), kind=kOutput, calls=%fused_computation.5 | convolution fusion | flops 3258968064 | bytes 54026240 | tf_op jit(solution)/shard_map/cond/branch_0_fun/skqd,rkd->kqsr/dot_general | solution.py:87
  72.5 22.0 %fusion.2 = f32[2,6,512]{2,1,0:T(8,128)S(1)} fusion(f32[2,2048,512,6]{2,1,3,0:T(8,128)} %get-tuple-element.47, f32[2,6,512]{2,1,0:T(8,128)S(1)} %get-tuple-element.46, pred[512,2048]{0,1:T(8,128)(4,1)S(1)} %iota_compare_fusion), kind=kLoop, calls=%fused_computation.7 | loop fusion | flops 62908416 | bytes 51429376 | tf_op jit(solution)/shard_map/cond/branch_0_fun/reduce_sum | solution.py:98
  94.4 0.3 reshape.73
  94.7 24.1 %fusion.6 = f32[2,6,512,128]{3,2,1,0:T(8,128)} fusion(f32[2,2048,512,6]{2,1,3,0:T(8,128)} %get-tuple-element.47, f32[2,6,512]{2,1,0:T(8,128)S(1)} %get-tuple-element.46, pred[512,2048]{0,1:T(8,128)(4,1)S(1)} %iota_compare_fusion, f32[2,6,512]{2,1,0:T(8,128)S(1)} %get-tuple-element.44, bf16[2048,2,128,1]{2,1,0,3:T(2,128)(2,1)S(1)} %bitcast.34), kind=kOutput, calls=%fused_computation.11 | convolution fusion | flops 3284926464 | bytes 55623680 | tf_op jit(solution)/shard_map/cond/branch_0_fun/kqsr,rkd->kqsd/dot_general | solution.py:99
  118.8 3.7 copy.38
  122.5 2.3 divide_convert_fusion
  124.8 15.7 %convolution_convert_fusion = bf16[512,6144]{1,0:T(8,128)(2,1)} fusion(bf16[512,1536]{0,1:T(8,128)(2,1)S(1)} %bitcast.33, bf16[1536,6144]{1,0:T(8,128)(2,1)} %param.18), kind=kOutput, calls=%fused_computation.22 | convolution fusion | flops 9666822144 | bytes 26738688 | tf_op jit(solution)/shard_map/dot_general | solution.py:116
  140.5 0.0 reduce-scatter.3.cloned.1.call-update
  140.6 0.0 all-gather.10.cloned.1.call-start
  140.6 110.8 %reduce-scatter.3.cloned.1.call-done = bf16[512,1536]{1,0:T(8,128)(2,1)} async-done(((bf16[512,6144]{1,0:T(8,128)(2,1)}), bf16[512,1536]{1,0:T(8,128)(2,1)}) %reduce-scatter.3.cloned.1.call-update) | async-done | bytes 1572880 | tf_op jit(solution)/shard_map/reduce_scatter | solution.py:117
  251.5 2.9 add_convert_fusion.1
  254.4 0.0 all-gather.10.cloned.1.call-update
  254.4 0.0 all-gather.12.cloned.1.call-start
  254.5 0.1 fusion.33
  254.6 46.9 %all-gather.10.cloned.1.call-done = bf16[2048,1536]{1,0:T(8,128)(2,1)} async-done(((bf16[512,1536]{1,0:T(8,128)(2,1)}), bf16[2048,1536]{1,0:T(8,128)(2,1)}) %all-gather.10.cloned.1.call-update) | async-done | bytes 6291472 | tf_op jit(solution)/shard_map/all_gather | solution.py:129
  301.5 11.4 %scatter_custom_fusion = bf16[640,1536]{1,0:T(8,128)(2,1)S(1)} fusion(s32[2048]{0:T(1024)S(1)} %bitcast.37, bf16[2048,1536]{1,0:T(8,128)(2,1)} %all-gather.10.cloned.1.call-done, bf16[]{:T(256)} %constant.49.clone.1), kind=kCustom, calls=%fused_computation.36 | custom fusion | bytes 1966592 | tf_op jit(solution)/shard_map/scatter | solution.py:129
  312.9 8.3 %convolution_convert_fusion.1 = bf16[640,2048]{1,0:T(8,128)(2,1)} fusion(bf16[1536,2048]{1,0:T(8,128)(2,1)} %param.22, bf16[640,1536]{1,0:T(8,128)(2,1)S(1)} %scatter_custom_fusion, f32[1536]{0:T(1024)S(1)} %convert_element_type.87), kind=kOutput, calls=%fused_computation.28 | convolution fusion | flops 4030791680 | bytes 10885120 | tf_op jit(solution)/shard_map/dot_general | solution.py:135
  321.2 0.0 all-gather.12.cloned.1.call-update
  321.2 0.0 all-reduce.4.cloned.1.call-start
  321.3 8.5 %convolution_convert_fusion.2 = bf16[640,2048]{1,0:T(8,128)(2,1)} fusion(bf16[1536,2048]{1,0:T(8,128)(2,1)} %param.21, bf16[640,1536]{1,0:T(8,128)(2,1)S(1)} %scatter_custom_fusion, f32[1536]{0:T(1024)S(1)} %convert_element_type.87), kind=kOutput, calls=%fused_computation.29 | convolution fusion | flops 4030791680 | bytes 10885120 | tf_op jit(solution)/shard_map/dot_general | solution.py:134
  329.8 0.0 all-reduce.4.cloned.1.call-update
  329.8 0.0 reduce-scatter.5.cloned.1.call-start
  329.8 8.0 %scatter_custom_fusion.1 = s32[640]{0:T(1024)S(1)} fusion(s32[2048]{0:T(1024)S(1)} %bitcast.38, s32[2048]{0:T(1024)S(1)} %get-tuple-element.40, s32[]{:T(128)} %constant.23.clone.1), kind=kCustom, calls=%fused_computation.54 | custom fusion | bytes 2564 | tf_op jit(solution)/shard_map/scatter | solution.py:23
  337.9 0.5 fusion.17
  338.4 0.6 fusion.23
  339.0 28.1 %all-reduce.1 = (bf16[640]{0:T(1024)(128)(2,1)S(1)}, bf16[640,8]{0,1:T(8,128)(2,1)S(1)}) all-reduce(bf16[640]{0:T(1024)(128)(2,1)S(1)} %fusion.17, bf16[640,8]{0,1:T(8,128)(2,1)S(1)} %fusion.23), channel_id=1, replica_groups=mesh['groups'=2,'wide'=4,'ctx'=4] {'wide'}, use_global_device_ids=true, to_apply=%region_9.10 | all-reduce | flops 5760 | bytes 23040 | tf_op jit(solution)/shard_map/psum | solution.py:140
  367.2 138.6 %all-gather.12.cloned.1.call-done = bf16[2560,2048]{1,0:T(8,128)(2,1)} async-done(((bf16[640,2048]{1,0:T(8,128)(2,1)}), bf16[2560,2048]{1,0:T(8,128)(2,1)}) %all-gather.12.cloned.1.call-update) | async-done | bytes 10485776 | tf_op jit(solution)/shard_map/all_gather | solution.py:139
  505.8 8.7 %reduce_sum.51 = bf16[640,2048]{1,0:T(8,128)(2,1)} reduce(bf16[4,640,2048]{2,1,0:T(8,128)(2,1)} %bitcast.30, bf16[]{:T(256)} %constant.49.clone.1), dimensions={0}, to_apply=%region_10.11 | reduce | flops 3932160 | bytes 13107202 | tf_op jit(solution)/shard_map/reduce_sum | solution.py:139
  514.5 95.9 %all-reduce.4.cloned.1.call-done = bf16[640,2048]{1,0:T(8,128)(2,1)} async-done(((bf16[640,2048]{1,0:T(8,128)(2,1)}), bf16[640,2048]{1,0:T(8,128)(2,1)}) %all-reduce.4.cloned.1.call-update) | async-done | bytes 2621456 | tf_op jit(solution)/shard_map/psum | solution.py:138
  610.3 9.2 %fusion.18 = bf16[640,1536]{1,0:T(8,128)(2,1)S(1)} fusion(bf16[2048,1536]{1,0:T(8,128)(2,1)} %param.23, bf16[640,2048]{1,0:T(8,128)(2,1)} %reduce_sum.51, bf16[640,2048]{1,0:T(8,128)(2,1)} %all-reduce.4.cloned.1.call-done, f32[640]{0:T(1024)S(1)} %divide_reduce_fusion, f32[640]{0:T(1024)S(1)} %add_rsqrt_fusion), kind=kOutput, calls=%fused_computation.33 | convolution fusion | flops 4040949760 | bytes 13505536 | tf_op jit(solution)/shard_map/dot_general | solution.py:144
  619.6 0.1 concatenate.3
  619.7 10.1 %gather_fusion = bf16[2048,1536]{1,0:T(8,128)(2,1)} fusion(bf16[641,1536]{1,0:T(8,128)(2,1)S(1)} %concatenate.3, s32[2048]{0:T(1024)S(1)} %broadcast_clamp_fusion), kind=kCustom, calls=%fused_computation | custom fusion | bytes 12591104 | tf_op jit(solution)/shard_map/jit(_take)/gather | solution.py:147
  629.8 6.6 select_convert_fusion
  636.4 58.0 %reduce-scatter.5.cloned.1.call-done = bf16[512,1536]{1,0:T(8,128)(2,1)} async-done(((bf16[2048,1536]{1,0:T(8,128)(2,1)}), bf16[512,1536]{1,0:T(8,128)(2,1)}) %reduce-scatter.5.cloned.1.call-update) | async-done | bytes 1572880 | tf_op jit(solution)/shard_map/reduce_scatter | solution.py:146
  694.4 2.9 add_convert_fusion
  (29 shorter events, 0.2 us)
Async XLA Ops:
  6.5 1.2 copy-start
  6.5 21.8 %all-gather.6.cloned.1.call-start = ((), (), s32[]{:S(2)}) async-start(), calls=%async_computation.2 | async-start | bytes 1310720 | tf_op jit(solution)/shard_map/all_gather | solution.py:78
  8.5 38.1 %all-gather.8.cloned.1.call-start = ((), (), s32[]{:S(2)}) async-start(), calls=%async_computation.3 | async-start | bytes 1310720 | tf_op jit(solution)/shard_map/all_gather | solution.py:79
  10.3 241.2 %reduce-scatter.3.cloned.1.call-start = ((), (), s32[]{:S(2)}) async-start(), calls=%async_computation.4 | async-start | bytes 7864320 | tf_op jit(solution)/shard_map/reduce_scatter | solution.py:117
  72.4 22.0 %copy-start.4 = (bf16[2048,256]{1,0:T(8,128)(2,1)S(1)}, bf16[2048,256]{1,0:T(8,128)(2,1)}, u32[]{:S(2)}) copy-start(bf16[2048,256]{1,0:T(8,128)(2,1)} %get-tuple-element.22) | copy-start | bytes 3145732 | tf_op jit(solution)/shard_map/cond
  140.5 111.0 %copy-start.3 = (bf16[512,1536]{1,0:T(8,128)(2,1)S(1)}, bf16[512,1536]{1,0:T(8,128)(2,1)}, u32[]{:S(2)}) copy-start(bf16[512,1536]{1,0:T(8,128)(2,1)} %param.17) | copy-start | bytes 4718596
  140.5 113.9 %copy-start.7 = (bf16[1536]{0:T(1024)(128)(2,1)S(1)}, bf16[1536]{0:T(1024)(128)(2,1)}, u32[]{:S(2)}) copy-start(bf16[1536]{0:T(1024)(128)(2,1)} %param.19) | copy-start | bytes 9220
  140.5 114.0 %copy-start.5 = (s32[2048,2]{0,1:T(2,128)S(1)}, s32[2048,2]{0,1:T(2,128)}, u32[]{:S(2)}) copy-start(s32[2048,2]{0,1:T(2,128)} %param.24) | copy-start | bytes 49156
  140.6 113.9 %copy-start.6 = (s32[2048,2]{0,1:T(2,128)S(1)}, s32[2048,2]{0,1:T(2,128)}, u32[]{:S(2)}) copy-start(s32[2048,2]{0,1:T(2,128)} %param.25) | copy-start | bytes 49156
  140.6 160.9 %all-gather.10.cloned.1.call-start = ((), (), s32[]{:S(2)}) async-start(), calls=%async_computation.5 | async-start | bytes 7864320 | tf_op jit(solution)/shard_map/all_gather | solution.py:129
  254.4 251.3 %all-gather.12.cloned.1.call-start = ((), (), s32[]{:S(2)}) async-start(), calls=%async_computation.8 | async-start | bytes 13107200 | tf_op jit(solution)/shard_map/all_gather | solution.py:139
  321.2 289.1 %all-reduce.4.cloned.1.call-start = ((), (), s32[]{:S(2)}) async-start(), calls=%async_computation.6 | async-start | bytes 5242880 | tf_op jit(solution)/shard_map/psum | solution.py:138
  329.8 8.6 %copy-start.8 = (bf16[1536,8]{0,1:T(8,128)(2,1)S(1)}, bf16[1536,8]{0,1:T(8,128)(2,1)}, u32[]{:S(2)}) copy-start(bf16[1536,8]{0,1:T(8,128)(2,1)} %param.20) | copy-start | bytes 73732
  329.8 364.7 %reduce-scatter.5.cloned.1.call-start = ((), (), s32[]{:S(2)}) async-start(), calls=%async_computation.7 | async-start | bytes 7864320 | tf_op jit(solution)/shard_map/reduce_scatter | solution.py:146
  636.4 58.0 %copy-start.2 = (bf16[512,1536]{1,0:T(8,128)(2,1)S(1)}, bf16[512,1536]{1,0:T(8,128)(2,1)}, u32[]{:S(2)}) copy-start(bf16[512,1536]{1,0:T(8,128)(2,1)} %add_convert_fusion.1) | copy-start | bytes 4718596
  636.4 61.0 %copy-start.1 = (bf16[512,1024]{1,0:T(8,128)(2,1)S(1)}, bf16[512,1024]{1,0:T(8,128)(2,1)}, u32[]{:S(2)}) copy-start(bf16[512,1024]{1,0:T(8,128)(2,1)} %param.15) | copy-start | bytes 3145732
Sparse Core Ops, SparseCore 0:
  8.9 19.4 all-gather.5
  29.9 16.6 all-gather.7
  140.7 110.7 reduce-scatter.2
  254.5 46.8 all-gather.9
  321.3 184.3 all-gather.11
  508.0 102.2 all-reduce.3
  636.5 57.8 reduce-scatter.4
